TPU v7x, 256 devices: a whole 4x4x8 slice. The times are simulated.
256 devices in a mesh: aa: 32 (over z, x), ba: 8 (over y, core).
Axes of the slice: x: 4, y: 4, z: 8, core: 2. Of those that a mesh axis runs over, the one named last changes fastest.
Arguments:
- snapshots: float32 [8192, 65536], P(('aa', 'ba')), may hold values from -125 to 125
Outputs:
- factors: float32 [8, 64, 64], replicated
- pod_modes: float32 [8, 64, 65536], P(None, None, ('aa', 'ba'))
All inputs are finite; a program needn't handle non-finite values.
Results may differ from a plain program's by a relative error of at most 0.000098.
Values sent between devices are 32-bit elements; how exact they have to be, the bound alone decides.
No kernel may reach another device: no remote copies, remote signals or barrier semaphores. Data moves between devices by JAX's collectives and lax.ppermute only.
A program may use at most 128 MiB of HBM per device.

v0:
```python
import math
import jax
import jax.numpy as jnp
from jax import lax
from jax.sharding import PartitionSpec as P

FREQS = 8


def spectral_table(block_len, points):
    sample = jnp.arange(block_len, dtype=jnp.int32)
    harmonic = jnp.arange(1, FREQS + 1, dtype=jnp.int32)
    phase_turns = (sample[:, None] * harmonic[None, :] % block_len).astype(jnp.float32) * (
        2.0 * math.pi / block_len
    )
    sample_angle = sample.astype(jnp.float32) * (2.0 * math.pi / block_len)
    window = 0.5 - 0.5 * jnp.cos(sample_angle)
    norm_scale = 1.0 / jnp.sqrt(points * jnp.sum(window * window))
    cosine = window[:, None] * jnp.cos(phase_turns) * norm_scale
    sine = -window[:, None] * jnp.sin(phase_turns) * norm_scale
    return jnp.stack([cosine, sine], axis=1)


def local(snapshots):
    time_dev, points = snapshots.shape
    n_aa = lax.axis_size("aa")
    n_ba = lax.axis_size("ba")
    pts_dev = points // (n_aa * n_ba)
    block_len = time_dev * n_ba
    table = spectral_table(block_len, points)
    regrouped = lax.all_to_all(
        lax.all_to_all(snapshots, "aa", split_axis=1, concat_axis=0, tiled=True),
        "ba",
        split_axis=1,
        concat_axis=0,
        tiled=True,
    )
    arranged = regrouped.reshape(n_ba, n_aa, time_dev, pts_dev)
    table_parts = table.reshape(n_ba, time_dev, 2, FREQS)
    spectra = jnp.einsum("uasp,usgf->agfp", arranged, table_parts, precision=lax.Precision.HIGHEST)
    blocks = spectra.shape[0]
    columns = 2 * blocks
    product = jnp.einsum("bgfp,chfp->fbgch", spectra, spectra, precision=lax.Precision.HIGHEST)
    gram_sum = lax.psum(product.reshape(FREQS, columns, columns), ("aa", "ba"))
    lower_factor = jnp.linalg.cholesky(gram_sum)
    identity = jnp.broadcast_to(jnp.eye(columns, dtype=gram_sum.dtype), lower_factor.shape)
    inverse = lax.linalg.triangular_solve(lower_factor, identity, left_side=True, lower=True)
    pod_modes = math.sqrt(points) * jnp.einsum(
        "fibg,bgfp->fip",
        inverse.reshape(FREQS, columns, blocks, 2),
        spectra,
        precision=lax.Precision.HIGHEST,
    )
    return (jnp.swapaxes(lower_factor, 1, 2), pod_modes)


def solution(mesh):
    placed = (P(("aa", "ba"), None),)
    return jax.shard_map(
        local,
        mesh=mesh,
        in_specs=placed,
        out_specs=(P(), P(None, None, ("aa", "ba"))),
        check_vma=False,
    )
```

profile of v0, /device:TPU:2, one launch (start us, length us, event | category | flops | bytes accessed | tf_op | source)
XLA Modules:
  0.0 675.1 jit_solution(12656147163398301146)
XLA Ops:
  7.2 4.0 copy.75
  11.1 196.8 %all_to_all.32 = f32[32,32,2048]{2,0,1:T(8,128)S(1)} all-to-all(f32[32,32,2048]{2,0,1:T(8,128)S(1)} %bitcast.46), channel_id=1, replica_groups=mesh['aa'=32,'ba'=8] {'aa'}, dimensions={1} | all-to-all | bytes 16777216 | tf_op jit(solution)/shard_map/all_to_all | solution.py:32
  207.9 4.1 copy.61
  212.0 5.8 copy.38
  217.8 5.0 all-to-all-start.1
  222.8 0.2 all-reduce.2.cloned.1.call-start
  223.0 0.6 multiply_reduce_fusion
  224.4 0.2 multiply_multiply_fusion.1
  224.7 92.7 %all-to-all-done.1 = f32[1024,8,256]{2,0,1:T(8,128)} async-done(((f32[1024,8,256]{2,0,1:T(8,128)}), f32[1024,8,256]{2,0,1:T(8,128)}, u32[]{:S(2)}, u32[]{:S(2)}) %all-to-all-start.1) | async-done | bytes 8388640 | tf_op jit(solution)/shard_map/all_to_all | solution.py:31
  317.4 9.1 %fusion = f32[2,8,32,256,1]{3,1,4,2,0:T(8,128)S(1)} fusion(f32[8,32,32,256]{3,2,1,0:T(8,128)} %bitcast.4, f32[8,32,1,8]{1,3,0,2:T(8,128)S(1)} %get-tuple-element.13, f32[8,32,1,8]{1,3,0,2:T(8,128)S(1)} %get-tuple-element.12), kind=kOutput, calls=%fused_computation.1 | convolution fusion | flops 402657280 | bytes 8929280 | tf_op jit(solution)/shard_map/uasp,usgf->agfp/dot_general | solution.py:40
  326.5 1.6 fusion.4
  328.1 1.2 copy.42
  329.3 1.9 copy.43
  331.2 0.0 all-reduce.2.cloned.1.call-update
  331.3 245.3 %all-reduce.2.cloned.1.call-done = f32[8,64,64]{1,2,0:T(8,128)} async-done(((f32[8,64,64]{1,2,0:T(8,128)}), f32[8,64,64]{1,2,0:T(8,128)}) %all-reduce.2.cloned.1.call-update) | async-done | bytes 131088 | tf_op jit(solution)/shard_map/psum | solution.py:44
  576.5 1.1 copy.44
  577.6 1.0 fusion.10
  578.6 46.9 %custom-call.7 = f32[8,64,64]{2,1,0:T(8,128)S(1)} custom-call(f32[8,64,64]{2,1,0:T(8,128)S(1)} %fusion.10), custom_call_target="Cholesky" | custom-call | tf_op jit(solution)/shard_map/jit(cholesky)/cholesky | solution.py:45
  625.5 0.1 compare_reduce_fusion
  625.7 0.1 select_bitcast_fusion
  625.8 0.8 copy.49
  626.6 39.3 %custom-call.8 = f32[8,1,64,64]{2,3,1,0:T(8,128)S(1)} custom-call(f32[8,1,64,64]{3,2,1,0:T(8,128)S(1)} %get-tuple-element.10), custom_call_target="InvertDiagBlocksLowerTriangular" | custom-call | tf_op jit(solution)/shard_map/triangular_solve | solution.py:47
  665.9 0.6 fusion.8
  666.5 0.1 copy.46
  666.7 1.6 fusion.3
  (7 shorter events, 0.1 us)
Async XLA Ops:
  217.8 99.6 %all-to-all-start.1 = ((f32[1024,8,256]{2,0,1:T(8,128)}), f32[1024,8,256]{2,0,1:T(8,128)}, u32[]{:S(2)}, u32[]{:S(2)}) async-start(f32[1024,8,256]{2,0,1:T(8,128)} %copy.38), calls=%async_computation.1 | async-start | bytes 16777216 | tf_op jit(solution)/shard_map/all_to_all | solution.py:31
  222.8 353.8 %all-reduce.2.cloned.1.call-start = ((), (), s32[]{:S(2)}) async-start(), calls=%async_computation.2 | async-start | bytes 524288 | tf_op jit(solution)/shard_map/psum | solution.py:44
Sparse Core Ops, SparseCore 0:
  331.4 245.1 all-reduce.1
where the time goes:
time: 675 us
  waiting for transfers between devices  338 us (50%)
  blocking collectives  197 us (29%)
  other arithmetic  88.4 us (13%)
  local copies, waits for them, and re-layouts  19 us (3%)
  between operations  14.8 us (2%)
  matrix products  12.9 us (2%)
    psum x1, waiting for transfers between devices, local(): gram_sum = lax.psum(product.reshape(FREQS, columns, columns), ('aa', 'ba'))  245 us
    all_to_all x1, blocking collectives, local(): lax.all_to_all(snapshots, 'aa', split_axis=1, concat_axis=0, tiled=True)  197 us
    all_to_all x1, waiting for transfers between devices, local(): lax.all_to_all(lax.all_to_all(snapshots, 'aa', split_axis=1, concat_axis=...  92.7 us
    another operation x4, other arithmetic, local(): lower_factor = jnp.linalg.cholesky(gram_sum)  47.1 us
    another operation x2, other arithmetic, local(): lax.linalg.triangular_solve(lower_factor, identity, left_side=True, lower...  39.4 us
  transfers between devices with their start and end apart: 2, of which 2 were waited for; matrix products, arithmetic and copies ran while one was open for 0% of the time, Pallas kernels for 0%

commit v1 on v0

--- a/solution.py
+++ b/solution.py
@@ -41,7 +41,8 @@
     blocks = spectra.shape[0]
     columns = 2 * blocks
     product = jnp.einsum("bgfp,chfp->fbgch", spectra, spectra, precision=lax.Precision.HIGHEST)
-    gram_sum = lax.psum(product.reshape(FREQS, columns, columns), ("aa", "ba"))
+    inner = lax.psum(product.reshape(FREQS, columns, columns), "aa")
+    gram_sum = lax.psum(inner, "ba")
     lower_factor = jnp.linalg.cholesky(gram_sum)
     identity = jnp.broadcast_to(jnp.eye(columns, dtype=gram_sum.dtype), lower_factor.shape)
     inverse = lax.linalg.triangular_solve(lower_factor, identity, left_side=True, lower=True)

time: 675 us -> 634 us (0.939)
  waiting for transfers between devices: 338 us -> 296 us
    psum x1 -> x2, waiting for transfers between devices: 245 us -> 203 us  [the longest x1 138 us: local(): inner = lax.psum(product.reshape(FREQS, columns, columns), 'aa')]
  transfers between devices with their start and end apart: 2 -> 3, of which waited for: 2 -> 3; matrix products, arithmetic and copies ran while one was open for 0% -> 0% of each run, Pallas kernels for 0% -> 0%
where the time goes in v1:
time: 634 us; the launch traced here: 633 us
  waiting for transfers between devices  296 us (47%)
  blocking collectives  197 us (31%)
  other arithmetic  88.4 us (14%)
  local copies, waits for them, and re-layouts  19 us (3%)
  between operations  14.8 us (2%)
  matrix products  12.9 us (2%)
    all_to_all x1, blocking collectives, local(): lax.all_to_all(snapshots, 'aa', split_axis=1, concat_axis=0, tiled=True)  197 us
    psum x1, waiting for transfers between devices, local(): inner = lax.psum(product.reshape(FREQS, columns, columns), 'aa')  138 us
    all_to_all x1, waiting for transfers between devices, local(): lax.all_to_all(lax.all_to_all(snapshots, 'aa', split_axis=1, concat_axis=...  92.7 us
    psum x1, waiting for transfers between devices, local(): gram_sum = lax.psum(inner, 'ba')  65.4 us
    another operation x4, other arithmetic, local(): lower_factor = jnp.linalg.cholesky(gram_sum)  47.1 us
    another operation x2, other arithmetic, local(): lax.linalg.triangular_solve(lower_factor, identity, left_side=True, lower...  39.4 us
  transfers between devices with their start and end apart: 3, of which 3 were waited for; matrix products, arithmetic and copies ran while one was open for 0% of the time, Pallas kernels for 0%

profile of v1, /device:TPU:2, one launch (start us, length us, event | category | flops | bytes accessed | tf_op | source)
XLA Modules:
  0.0 633.2 jit_solution(1364482919001259132)
XLA Ops:
  7.2 4.0 copy.75
  11.1 196.8 %all_to_all.32 = f32[32,32,2048]{2,0,1:T(8,128)S(1)} all-to-all(f32[32,32,2048]{2,0,1:T(8,128)S(1)} %bitcast.46), channel_id=1, replica_groups=mesh['aa'=32,'ba'=8] {'aa'}, dimensions={1} | all-to-all | bytes 16777216 | tf_op jit(solution)/shard_map/all_to_all | solution.py:32
  207.9 4.1 copy.61
  212.0 5.8 copy.38
  217.8 5.0 all-to-all-start.1
  222.8 0.2 all-reduce.3.cloned.1.call-start
  223.0 0.6 multiply_reduce_fusion
  224.4 0.2 multiply_multiply_fusion.1
  224.6 92.7 %all-to-all-done.1 = f32[1024,8,256]{2,0,1:T(8,128)} async-done(((f32[1024,8,256]{2,0,1:T(8,128)}), f32[1024,8,256]{2,0,1:T(8,128)}, u32[]{:S(2)}, u32[]{:S(2)}) %all-to-all-start.1) | async-done | bytes 8388640 | tf_op jit(solution)/shard_map/all_to_all | solution.py:31
  317.4 9.1 %fusion = f32[2,8,32,256,1]{3,1,4,2,0:T(8,128)S(1)} fusion(f32[8,32,32,256]{3,2,1,0:T(8,128)} %bitcast.4, f32[8,32,1,8]{1,3,0,2:T(8,128)S(1)} %get-tuple-element.13, f32[8,32,1,8]{1,3,0,2:T(8,128)S(1)} %get-tuple-element.12), kind=kOutput, calls=%fused_computation.1 | convolution fusion | flops 402657280 | bytes 8929280 | tf_op jit(solution)/shard_map/uasp,usgf->agfp/dot_general | solution.py:40
  326.5 1.6 fusion.4
  328.1 1.2 copy.42
  329.3 1.9 copy.43
  331.2 0.0 all-reduce.3.cloned.1.call-update
  331.2 0.0 all-reduce.5.cloned.1.call-start
  331.3 137.8 %all-reduce.3.cloned.1.call-done = f32[8,64,64]{1,2,0:T(8,128)} async-done(((f32[8,64,64]{1,2,0:T(8,128)}), f32[8,64,64]{1,2,0:T(8,128)}) %all-reduce.3.cloned.1.call-update) | async-done | bytes 131088 | tf_op jit(solution)/shard_map/psum | solution.py:44
  469.2 0.0 all-reduce.5.cloned.1.call-update
  469.2 65.4 %all-reduce.5.cloned.1.call-done = f32[8,64,64]{1,2,0:T(8,128)} async-done(((f32[8,64,64]{1,2,0:T(8,128)}), f32[8,64,64]{1,2,0:T(8,128)}) %all-reduce.5.cloned.1.call-update) | async-done | bytes 131088 | tf_op jit(solution)/shard_map/psum | solution.py:45
  534.6 1.1 copy.44
  535.7 1.0 fusion.10
  536.7 46.9 %custom-call.7 = f32[8,64,64]{2,1,0:T(8,128)S(1)} custom-call(f32[8,64,64]{2,1,0:T(8,128)S(1)} %fusion.10), custom_call_target="Cholesky" | custom-call | tf_op jit(solution)/shard_map/jit(cholesky)/cholesky | solution.py:46
  583.6 0.1 compare_reduce_fusion
  583.8 0.1 select_bitcast_fusion
  583.9 0.8 copy.49
  584.7 39.3 %custom-call.8 = f32[8,1,64,64]{2,3,1,0:T(8,128)S(1)} custom-call(f32[8,1,64,64]{3,2,1,0:T(8,128)S(1)} %get-tuple-element.10), custom_call_target="InvertDiagBlocksLowerTriangular" | custom-call | tf_op jit(solution)/shard_map/triangular_solve | solution.py:48
  624.0 0.6 fusion.8
  624.6 0.1 copy.46
  624.8 1.6 fusion.3
  (7 shorter events, 0.1 us)
Async XLA Ops:
  217.8 99.6 %all-to-all-start.1 = ((f32[1024,8,256]{2,0,1:T(8,128)}), f32[1024,8,256]{2,0,1:T(8,128)}, u32[]{:S(2)}, u32[]{:S(2)}) async-start(f32[1024,8,256]{2,0,1:T(8,128)} %copy.38), calls=%async_computation.1 | async-start | bytes 16777216 | tf_op jit(solution)/shard_map/all_to_all | solution.py:31
  222.8 246.4 %all-reduce.3.cloned.1.call-start = ((), (), s32[]{:S(2)}) async-start(), calls=%async_computation.2 | async-start | bytes 524288 | tf_op jit(solution)/shard_map/psum | solution.py:44
  331.2 203.4 %all-reduce.5.cloned.1.call-start = ((), (), s32[]{:S(2)}) async-start(), calls=%async_computation.3 | async-start | bytes 524288 | tf_op jit(solution)/shard_map/psum | solution.py:45
Sparse Core Ops, SparseCore 0:
  331.4 137.7 all-reduce.2
  471.5 63.1 all-reduce.4
